TPU v7x, 512 devices: a whole 4x4x16 slice. The times are simulated.
512 devices in a mesh: comp: 32 (over z, core), feat: 16 (over x, y).
Axes of the slice: x: 4, y: 4, z: 16, core: 2. Of those that a mesh axis runs over, the one named last changes fastest.
Arguments:
- block_values: bfloat16 [32, 16, 24, 128, 128], P('comp', 'feat'), may hold values from -0.0625 to 0.0625
- block_rows: int32 [32, 16, 24], P('comp', 'feat'), may hold values from 0 to 15, as said below
- block_cols: int32 [32, 16, 24], P('comp', 'feat'), may hold values from 0 to 13, as said below
- block_counts: int32 [32, 16], P('comp', 'feat'), may hold values from 8 to 24, as said below
- right_side: float32 [65536, 128], P(('comp', 'feat')), may hold values from -6 to 6
- ridge: float32 [128], replicated, may hold values from 0.1 to 2
Outputs:
- solution: float32 [28672, 128], P('feat')
- residual: float32 [65536, 128], P(('comp', 'feat'))
Inputs may be any that keep to these rules, and one draw needn't show every extreme that they name: Within one device the listed (block_rows, block_cols) pairs of all 24 slots are distinct; block rows are very uneven in how many blocks they hold. `block_cols`: see block_rows. `block_counts`: slots at or beyond a device's count are ignored; some device is full in every draw.
All inputs are finite; a program needn't handle non-finite values.
Results may differ from a plain program's by a relative error of at most 0.0029.
Values may be sent and summed in bfloat16 or wider, within the bound.
No kernel may reach another device: no remote copies, remote signals or barrier semaphores. Data moves between devices by JAX's collectives and lax.ppermute only.
A program may use at most 64 MiB of HBM per device.

v0:
```python
import jax
import jax.numpy as jnp
from jax import lax
from jax.sharding import PartitionSpec as P

RB_DEV = 16
CB_DEV = 14
ITERS = 2


def reduce_over(partial, axis, parts):
    rows = partial.shape[0] // parts
    pieces = partial.reshape(parts, rows, *partial.shape[1:])
    return lax.all_to_all(pieces, axis, 0, 0, tiled=True).sum(0)


def total_over_mesh(stacked, n_comp, n_feat):
    spread = jnp.broadcast_to(stacked[None], (n_feat,) + stacked.shape)
    by_feat = lax.all_to_all(spread, "feat", 0, 0, tiled=True).sum(0)
    spread = jnp.broadcast_to(by_feat[None], (n_comp,) + stacked.shape)
    return lax.all_to_all(spread, "comp", 0, 0, tiled=True).sum(0)


def shards(block_values, block_rows, block_cols, block_counts, right_side, ridge, n_comp, n_feat):
    values = block_values[0, 0]
    slot_rows = block_rows[0, 0]
    slot_cols = block_cols[0, 0]
    count_of_slots = block_counts[0, 0]
    responses = right_side.shape[1]
    total_slot_number = values.shape[0]
    block_edge = values.shape[1]
    feat_rows = CB_DEV * block_edge
    own_rows = feat_rows // n_comp
    comp_index = lax.axis_index("comp")
    slot_live = (jnp.arange(total_slot_number) < count_of_slots).astype(jnp.float32)
    row_lookup_table = (jnp.arange(RB_DEV)[:, None] == slot_rows[None, :]).astype(
        jnp.float32
    ) * slot_live[None, :]
    col_table = (jnp.arange(CB_DEV)[:, None] == slot_cols[None, :]).astype(jnp.float32) * slot_live[
        None, :
    ]

    def backward(low_slab):
        row_slabs = low_slab.reshape(RB_DEV, block_edge, responses)
        selected = jnp.take(row_slabs, slot_rows, axis=0)
        block_products = jnp.einsum(
            "sij,sik->sjk", values, selected, preferred_element_type=jnp.float32
        )
        summed = jnp.einsum(
            "qs,sjk->qjk", col_table, block_products, precision=lax.Precision.HIGHEST
        )
        return summed.reshape(feat_rows, responses)

    def forward(direction):
        col_panels = direction.astype(jnp.bfloat16).reshape(CB_DEV, block_edge, responses)
        forward_selected = jnp.take(col_panels, slot_cols, axis=0)
        forward_block_products = jnp.einsum(
            "sij,sjk->sik", values, forward_selected, preferred_element_type=jnp.float32
        )
        forward_summed = jnp.einsum(
            "rs,sik->rik", row_lookup_table, forward_block_products, precision=lax.Precision.HIGHEST
        )
        return reduce_over(forward_summed.reshape(RB_DEV * block_edge, responses), "feat", n_feat)

    def slab_of(current):
        return lax.all_gather(current.astype(jnp.bfloat16), "feat", axis=0, tiled=True)

    def gradient_rows(current):
        return reduce_over(backward(slab_of(current)), "comp", n_comp)

    def own_part(full):
        return lax.dynamic_slice_in_dim(full, comp_index * own_rows, own_rows, axis=0)

    def col_sq(x):
        return jnp.sum(x * x, axis=0)

    residual = right_side
    gradient_own = gradient_rows(residual)
    direction = lax.all_gather(gradient_own, "comp", axis=0, tiled=True)
    image_rows = forward(direction)
    energy, image_energy = total_over_mesh(
        jnp.stack([col_sq(gradient_own), col_sq(image_rows)]), n_comp, n_feat
    )
    step_size = energy / (image_energy + ridge * energy)
    solution = step_size * direction
    residual = residual - step_size * image_rows
    for _ in range(1, ITERS):
        gradient_own = gradient_rows(residual) - ridge * own_part(solution)
        gathered = lax.all_gather(
            jnp.concatenate([gradient_own, col_sq(gradient_own)[None]], axis=0),
            "comp",
            axis=0,
            tiled=False,
        )
        gradient = gathered[:, :own_rows].reshape(feat_rows, responses)
        comp_energy = jnp.sum(gathered[:, own_rows], axis=0)
        spread = jnp.broadcast_to(comp_energy[None, None], (n_feat, 1, responses))
        next_energy = lax.all_to_all(spread, "feat", 0, 0, tiled=True).sum(0)[0]
        direction = gradient + next_energy / energy * direction
        energy = next_energy
        image_rows = forward(direction)
        image_energy, direction_energy = total_over_mesh(
            jnp.stack([col_sq(image_rows), col_sq(own_part(direction))]), n_comp, n_feat
        )
        step_size = energy / (image_energy + ridge * direction_energy)
        solution = solution + step_size * direction
        residual = residual - step_size * image_rows
    return (solution, residual)


def solution(mesh):
    placed = (
        P("comp", "feat", None, None, None),
        P("comp", "feat", None),
        P("comp", "feat", None),
        P("comp", "feat"),
        P(("comp", "feat"), None),
        P(),
    )
    n_comp = mesh.shape["comp"]
    n_feat = mesh.shape["feat"]

    def body(*args):
        return shards(*args, n_comp=n_comp, n_feat=n_feat)

    return jax.shard_map(
        body,
        mesh=mesh,
        in_specs=placed,
        out_specs=(P("feat", None), P(("comp", "feat"), None)),
        check_vma=False,
    )
```

profile of v0, /device:TPU:1, one launch (start us, length us, event | category | flops | bytes accessed | tf_op | source)
XLA Modules:
  0.0 376.8 jit_solution(10062302333413157449)
XLA Ops:
  3.6 20.0 %all_gather.15 = bf16[2048,128]{1,0:T(8,128)(2,1)S(1)} all-gather(bf16[128,128]{1,0:T(8,128)(2,1)S(1)} %convert_element_type.22), channel_id=1, replica_groups=mesh['comp'=32,'feat'=16] {'feat'}, dimensions={0}, use_global_device_ids=true | all-gather | bytes 557056 | tf_op jit(solution)/shard_map/all_gather | solution.py:66
  24.2 1.7 convolution_bitcast_fusion.3
  25.9 2.0 copy.43
  28.9 1.2 copy.44
  30.1 21.0 %all-to-all-start = ((f32[32,56,128]{2,1,0:T(8,128)}), f32[32,56,128]{2,1,0:T(8,128)S(1)}, u32[]{:S(2)}, u32[]{:S(2)}) async-start(f32[32,56,128]{2,1,0:T(8,128)} %bitcast.7), calls=%async_computation | async-start | bytes 1835008 | tf_op jit(solution)/shard_map/all_to_all | solution.py:14
  51.2 50.2 %all-to-all-done = f32[32,56,128]{2,1,0:T(8,128)S(1)} async-done(((f32[32,56,128]{2,1,0:T(8,128)}), f32[32,56,128]{2,1,0:T(8,128)S(1)}, u32[]{:S(2)}, u32[]{:S(2)}) %all-to-all-start) | async-done | bytes 917536 | tf_op jit(solution)/shard_map/all_to_all | solution.py:14
  101.4 29.7 %all_gather.16 = f32[1792,128]{1,0:T(8,128)S(1)} all-gather(f32[56,128]{1,0:T(8,128)S(1)} %reduce_sum.137), channel_id=1, replica_groups=mesh['comp'=32,'feat'=16] {'comp'}, dimensions={0}, use_global_device_ids=true | all-gather | bytes 946176 | tf_op jit(solution)/shard_map/all_gather | solution.py:79
  131.9 2.0 convolution_bitcast_fusion.2
  133.9 2.0 copy.46
  136.9 1.3 copy.47
  138.2 4.8 %all-to-all-start.1 = ((f32[16,128,128]{2,1,0:T(8,128)}), f32[16,128,128]{2,1,0:T(8,128)S(1)}, u32[]{:S(2)}, u32[]{:S(2)}) async-start(f32[16,128,128]{2,1,0:T(8,128)} %copy.47), calls=%async_computation.1 | async-start | bytes 2097152 | tf_op jit(solution)/shard_map/all_to_all | solution.py:14
  143.1 16.0 %all-to-all-done.1 = f32[16,128,128]{2,1,0:T(8,128)S(1)} async-done(((f32[16,128,128]{2,1,0:T(8,128)}), f32[16,128,128]{2,1,0:T(8,128)S(1)}, u32[]{:S(2)}, u32[]{:S(2)}) %all-to-all-start.1) | async-done | bytes 1048608 | tf_op jit(solution)/shard_map/all_to_all | solution.py:14
  159.2 10.6 %all_to_all.45 = f32[16,2,128]{2,1,0:T(2,128)S(1)} all-to-all(f32[16,2,128]{2,1,0:T(2,128)S(1)} %broadcast_in_dim.30), channel_id=1, replica_groups=mesh['comp'=32,'feat'=16] {'feat'}, dimensions={0} | all-to-all | bytes 32768 | tf_op jit(solution)/shard_map/all_to_all | solution.py:19
  169.9 19.7 %all_to_all.46 = f32[32,2,128]{2,1,0:T(2,128)S(1)} all-to-all(f32[32,2,128]{2,1,0:T(2,128)S(1)} %broadcast_in_dim.31), channel_id=1, replica_groups=mesh['comp'=32,'feat'=16] {'comp'}, dimensions={0} | all-to-all | bytes 65536 | tf_op jit(solution)/shard_map/all_to_all | solution.py:21
  189.6 16.7 %all_gather.17 = bf16[2048,128]{1,0:T(8,128)(2,1)S(1)} all-gather(bf16[128,128]{1,0:T(8,128)(2,1)S(1)} %fusion.16), channel_id=1, replica_groups=mesh['comp'=32,'feat'=16] {'feat'}, dimensions={0}, use_global_device_ids=true | all-gather | bytes 557056 | tf_op jit(solution)/shard_map/all_gather | solution.py:66
  207.0 1.7 convolution_bitcast_fusion.1
  208.7 2.0 copy.51
  211.7 1.2 copy.52
  212.9 10.1 %all-to-all-start.4 = ((f32[32,56,128]{2,1,0:T(8,128)}), f32[32,56,128]{2,1,0:T(8,128)S(1)}, u32[]{:S(2)}, u32[]{:S(2)}) async-start(f32[32,56,128]{2,1,0:T(8,128)} %bitcast.17), calls=%async_computation.4 | async-start | bytes 1835008 | tf_op jit(solution)/shard_map/all_to_all | solution.py:14
  224.0 49.3 %all-to-all-done.4 = f32[32,56,128]{2,1,0:T(8,128)S(1)} async-done(((f32[32,56,128]{2,1,0:T(8,128)}), f32[32,56,128]{2,1,0:T(8,128)S(1)}, u32[]{:S(2)}, u32[]{:S(2)}) %all-to-all-start.4) | async-done | bytes 917536 | tf_op jit(solution)/shard_map/all_to_all | solution.py:14
  274.1 30.6 %all-gather.1 = f32[32,57,128]{2,1,0:T(8,128)S(1)} all-gather(f32[1,57,128]{2,1,0:T(8,128)S(1)} %maximum_bitcast_fusion), channel_id=2, replica_groups=mesh['comp'=32,'feat'=16] {'comp'}, dimensions={0}, use_global_device_ids=true | all-gather | bytes 963072 | tf_op jit(solution)/shard_map/all_gather | solution.py:89
  305.4 4.0 %all-to-all-start.5 = ((f32[16,1,128]{2,1,0:T(1,128)}), f32[16,1,128]{2,1,0:T(1,128)S(1)}, u32[]{:S(2)}, u32[]{:S(2)}) async-start(f32[16,1,128]{2,1,0:T(1,128)} %broadcast_in_dim.33), calls=%async_computation.5 | async-start | bytes 16384 | tf_op jit(solution)/shard_map/all_to_all | solution.py:98
  310.4 5.3 %all-to-all-done.5 = f32[16,1,128]{2,1,0:T(1,128)S(1)} async-done(((f32[16,1,128]{2,1,0:T(1,128)}), f32[16,1,128]{2,1,0:T(1,128)S(1)}, u32[]{:S(2)}, u32[]{:S(2)}) %all-to-all-start.5) | async-done | bytes 8224 | tf_op jit(solution)/shard_map/all_to_all | solution.py:98
  315.8 2.2 fusion.53
  318.7 2.0 convolution_bitcast_fusion
  320.7 2.0 copy.55
  323.7 1.3 copy.56
  325.0 3.7 all-to-all-start.6
  329.4 14.4 %all-to-all-done.6 = f32[16,128,128]{2,1,0:T(8,128)S(1)} async-done(((f32[16,128,128]{2,1,0:T(8,128)}), f32[16,128,128]{2,1,0:T(8,128)S(1)}, u32[]{:S(2)}, u32[]{:S(2)}) %all-to-all-start.6) | async-done | bytes 1048608 | tf_op jit(solution)/shard_map/all_to_all | solution.py:14
  344.0 10.1 %all_to_all.47 = f32[16,2,128]{2,1,0:T(2,128)S(1)} all-to-all(f32[16,2,128]{2,1,0:T(2,128)S(1)} %broadcast_in_dim.34), channel_id=1, replica_groups=mesh['comp'=32,'feat'=16] {'feat'}, dimensions={0} | all-to-all | bytes 32768 | tf_op jit(solution)/shard_map/all_to_all | solution.py:19
  354.2 19.7 %all_to_all.48 = f32[32,2,128]{2,1,0:T(2,128)S(1)} all-to-all(f32[32,2,128]{2,1,0:T(2,128)S(1)} %broadcast_in_dim.35), channel_id=1, replica_groups=mesh['comp'=32,'feat'=16] {'comp'}, dimensions={0} | all-to-all | bytes 65536 | tf_op jit(solution)/shard_map/all_to_all | solution.py:21
  374.0 2.2 multiply_add_fusion
  (57 shorter events, 14.7 us)
Async XLA Ops:
  0.6 23.6 %copy-start = (bf16[1,1,24,128,128]{4,3,2,1,0:T(8,128)(2,1)S(1)}, bf16[1,1,24,128,128]{4,3,2,1,0:T(8,128)(2,1)}, u32[]{:S(2)}) copy-start(bf16[1,1,24,128,128]{4,3,2,1,0:T(8,128)(2,1)} %param.10) | copy-start | bytes 2359300
  25.9 2.0 copy-start.3
  30.1 71.2 %all-to-all-start = ((f32[32,56,128]{2,1,0:T(8,128)}), f32[32,56,128]{2,1,0:T(8,128)S(1)}, u32[]{:S(2)}, u32[]{:S(2)}) async-start(f32[32,56,128]{2,1,0:T(8,128)} %bitcast.7), calls=%async_computation | async-start | bytes 1835008 | tf_op jit(solution)/shard_map/all_to_all | solution.py:14
  133.9 2.0 copy-start.4
  138.2 51.4 %copy-start.2 = (f32[128]{0:T(128)S(1)}, f32[128]{0:T(128)}, u32[]{:S(2)}) copy-start(f32[128]{0:T(128)} %param.15) | copy-start | bytes 1540
  138.2 51.4 %copy-start.1 = (f32[128,128]{1,0:T(8,128)S(1)}, f32[128,128]{1,0:T(8,128)}, u32[]{:S(2)}) copy-start(f32[128,128]{1,0:T(8,128)} %param.14) | copy-start | bytes 196612
  138.2 20.9 %all-to-all-start.1 = ((f32[16,128,128]{2,1,0:T(8,128)}), f32[16,128,128]{2,1,0:T(8,128)S(1)}, u32[]{:S(2)}, u32[]{:S(2)}) async-start(f32[16,128,128]{2,1,0:T(8,128)} %copy.47), calls=%async_computation.1 | async-start | bytes 2097152 | tf_op jit(solution)/shard_map/all_to_all | solution.py:14
  212.9 60.4 %all-to-all-start.4 = ((f32[32,56,128]{2,1,0:T(8,128)}), f32[32,56,128]{2,1,0:T(8,128)S(1)}, u32[]{:S(2)}, u32[]{:S(2)}) async-start(f32[32,56,128]{2,1,0:T(8,128)} %bitcast.17), calls=%async_computation.4 | async-start | bytes 1835008 | tf_op jit(solution)/shard_map/all_to_all | solution.py:14
  305.4 10.4 %all-to-all-start.5 = ((f32[16,1,128]{2,1,0:T(1,128)}), f32[16,1,128]{2,1,0:T(1,128)S(1)}, u32[]{:S(2)}, u32[]{:S(2)}) async-start(f32[16,1,128]{2,1,0:T(1,128)} %broadcast_in_dim.33), calls=%async_computation.5 | async-start | bytes 16384 | tf_op jit(solution)/shard_map/all_to_all | solution.py:98
  325.0 18.9 %all-to-all-start.6 = ((f32[16,128,128]{2,1,0:T(8,128)}), f32[16,128,128]{2,1,0:T(8,128)S(1)}, u32[]{:S(2)}, u32[]{:S(2)}) async-start(f32[16,128,128]{2,1,0:T(8,128)} %copy.56), calls=%async_computation.6 | async-start | bytes 2097152 | tf_op jit(solution)/shard_map/all_to_all | solution.py:14
where the time goes:
time: 378 us; the launch traced here: 377 us
  blocking collectives  157 us (42%)
  waiting for transfers between devices  135 us (36%)
  starting transfers between devices  43.7 us (12%)
  local copies, waits for them, and re-layouts  17.3 us (5%)
  matrix products  11.4 us (3%)
  other arithmetic  10.5 us (3%)
    all_to_all x4, waiting for transfers between devices, reduce_over(): return lax.all_to_all(pieces, axis, 0, 0, tiled=True).sum(0)  130 us
    all_to_all x4, starting transfers between devices, reduce_over(): return lax.all_to_all(pieces, axis, 0, 0, tiled=True).sum(0)  39.6 us
    all_to_all x2, blocking collectives, total_over_mesh(): return lax.all_to_all(spread, 'comp', 0, 0, tiled=True).sum(0)  39.4 us
    all_gather x2, blocking collectives, slab_of(): lax.all_gather(current.astype(jnp.bfloat16), 'feat', axis=0, tiled=True)  36.6 us
    all_gather x1, blocking collectives, shards(): lax.all_gather(jnp.concatenate([gradient_own, col_sq(gradient_own)[None]]...  30.6 us
    all_gather x1, blocking collectives, shards(): direction = lax.all_gather(gradient_own, 'comp', axis=0, tiled=True)  29.7 us
    all_to_all x2, blocking collectives, total_over_mesh(): by_feat = lax.all_to_all(spread, 'feat', 0, 0, tiled=True).sum(0)  20.8 us
  transfers between devices with their start and end apart: 5, of which 5 were waited for; matrix products, arithmetic and copies ran while one was open for 1% of the time, Pallas kernels for 0%

commit v1 on v0

--- a/solution.py
+++ b/solution.py
@@ -6,6 +6,22 @@
 RB_DEV = 16
 CB_DEV = 14
 ITERS = 2
+
+
+def ring_gather(x, axis, dim):
+    ways, here, step = (lax.axis_size(axis), lax.axis_index(axis), x.shape[dim])
+    lengths = [n * ways if d == dim else n for d, n in enumerate(x.shape)]
+    full = lax.dynamic_update_slice_in_dim(jnp.zeros(lengths, x.dtype), x, here * step, axis=dim)
+    going_up = going_down = x
+    for far in range(1, ways // 2 + 1):
+        going_up = lax.ppermute(going_up, axis, [(d, (d + 1) % ways) for d in range(ways)])
+        full = lax.dynamic_update_slice_in_dim(full, going_up, (here - far) % ways * step, axis=dim)
+        if 2 * far < ways:
+            going_down = lax.ppermute(going_down, axis, [(d, (d - 1) % ways) for d in range(ways)])
+            full = lax.dynamic_update_slice_in_dim(
+                full, going_down, (here + far) % ways * step, axis=dim
+            )
+    return full
 
 
 def reduce_over(partial, axis, parts):
@@ -63,7 +79,7 @@
         return reduce_over(forward_summed.reshape(RB_DEV * block_edge, responses), "feat", n_feat)
 
     def slab_of(current):
-        return lax.all_gather(current.astype(jnp.bfloat16), "feat", axis=0, tiled=True)
+        return ring_gather(current.astype(jnp.bfloat16), "feat", 0)
 
     def gradient_rows(current):
         return reduce_over(backward(slab_of(current)), "comp", n_comp)

time: 378 us -> 479 us (1.27)
  starting transfers between devices: 43.7 us -> 167 us
  blocking collectives: 157 us -> 119 us
  waiting for transfers between devices: 135 us -> 148 us
    ppermute x0 -> x30, starting transfers between devices: none -> 125 us  [the longest x14 92.1 us: ring_gather(): lax.ppermute(going_down, axis, [(d, (d - 1) % ways) for d in range(ways)])]
    all_gather x2 -> x0, blocking collectives: 36.6 us -> none  [slab_of(): lax.all_gather(current.astype(jnp.bfloat16), 'feat', axis=0, tiled=True)]
    ppermute x0 -> x30, waiting for transfers between devices: none -> 11.9 us  [the longest x16 11.9 us: ring_gather(): lax.ppermute(going_up, axis, [(d, (d + 1) % ways) for d in range(ways)])]
  transfers between devices with their start and end apart: 5 -> 35, of which waited for: 5 -> 7; matrix products, arithmetic and copies ran while one was open for 1% -> 1% of each run, Pallas kernels for 0% -> 0%
where the time goes in v1:
time: 479 us; the launch traced here: 477 us
  starting transfers between devices  167 us (35%)
  waiting for transfers between devices  148 us (31%)
  blocking collectives  119 us (25%)
  local copies, waits for them, and re-layouts  17.9 us (4%)
  matrix products  11.4 us (2%)
  other arithmetic  10.6 us (2%)
    all_to_all x4, waiting for transfers between devices, reduce_over(): return lax.all_to_all(pieces, axis, 0, 0, tiled=True).sum(0)  131 us
    ppermute x14, starting transfers between devices, ring_gather(): lax.ppermute(going_down, axis, [(d, (d - 1) % ways) for d in range(ways)])  92.1 us
    all_to_all x2, blocking collectives, total_over_mesh(): return lax.all_to_all(spread, 'comp', 0, 0, tiled=True).sum(0)  39.1 us
    all_to_all x4, starting transfers between devices, reduce_over(): return lax.all_to_all(pieces, axis, 0, 0, tiled=True).sum(0)  38 us
    ppermute x16, starting transfers between devices, ring_gather(): lax.ppermute(going_up, axis, [(d, (d + 1) % ways) for d in range(ways)])  33.3 us
    all_gather x1, blocking collectives, shards(): lax.all_gather(jnp.concatenate([gradient_own, col_sq(gradient_own)[None]]...  30.6 us
    all_gather x1, blocking collectives, shards(): direction = lax.all_gather(gradient_own, 'comp', axis=0, tiled=True)  29.7 us
    all_to_all x2, blocking collectives, total_over_mesh(): by_feat = lax.all_to_all(spread, 'feat', 0, 0, tiled=True).sum(0)  19.7 us
  transfers between devices with their start and end apart: 35, of which 7 were waited for; matrix products, arithmetic and copies ran while one was open for 1% of the time, Pallas kernels for 0%

profile of v1, /device:TPU:1, one launch (start us, length us, event | category | flops | bytes accessed | tf_op | source)
XLA Modules:
  0.0 476.8 jit_solution(12586926922955454531)
XLA Ops:
  1.6 4.0 collective-permute-start
  5.7 5.6 %collective-permute-start.1 = (bf16[128,128]{1,0:T(8,128)(2,1)S(1)}, bf16[128,128]{1,0:T(8,128)(2,1)S(1)}, u32[]{:S(2)}, u32[]{:S(2)}) collective-permute-start(bf16[128,128]{1,0:T(8,128)(2,1)S(1)} %get-tuple-element.11), channel_id=1, source_target_pairs={{0,15},{1,0},{2,1},{3,2},{4,3},{5,4},{6,5},{7,6},{8,7},{9,8},{10,9... | collective-permute-start | bytes 98312 | tf_op jit(solution)/shard_map/ppermute | solution.py:20
  15.5 6.7 %collective-permute-start.3 = (bf16[128,128]{1,0:T(8,128)(2,1)S(1)}, bf16[128,128]{1,0:T(8,128)(2,1)S(1)}, u32[]{:S(2)}, u32[]{:S(2)}) collective-permute-start(bf16[128,128]{1,0:T(8,128)(2,1)S(1)} %collective-permute-done.1), channel_id=1, source_target_pairs={{0,15},{1,0},{2,1},{3,2},{4,3},{5,4},{6,5},{7,6},{8,7},{9,8},{10,9... | collective-permute-start | bytes 98312 | tf_op jit(solution)/shard_map/ppermute | solution.py:20
  24.2 6.7 %collective-permute-start.5 = (bf16[128,128]{1,0:T(8,128)(2,1)S(1)}, bf16[128,128]{1,0:T(8,128)(2,1)S(1)}, u32[]{:S(2)}, u32[]{:S(2)}) collective-permute-start(bf16[128,128]{1,0:T(8,128)(2,1)S(1)} %collective-permute-done.3), channel_id=1, source_target_pairs={{0,15},{1,0},{2,1},{3,2},{4,3},{5,4},{6,5},{7,6},{8,7},{9,8},{10,9... | collective-permute-start | bytes 98312 | tf_op jit(solution)/shard_map/ppermute | solution.py:20
  32.8 6.7 %collective-permute-start.7 = (bf16[128,128]{1,0:T(8,128)(2,1)S(1)}, bf16[128,128]{1,0:T(8,128)(2,1)S(1)}, u32[]{:S(2)}, u32[]{:S(2)}) collective-permute-start(bf16[128,128]{1,0:T(8,128)(2,1)S(1)} %collective-permute-done.5), channel_id=1, source_target_pairs={{0,15},{1,0},{2,1},{3,2},{4,3},{5,4},{6,5},{7,6},{8,7},{9,8},{10,9... | collective-permute-start | bytes 98312 | tf_op jit(solution)/shard_map/ppermute | solution.py:20
  41.5 6.7 %collective-permute-start.9 = (bf16[128,128]{1,0:T(8,128)(2,1)S(1)}, bf16[128,128]{1,0:T(8,128)(2,1)S(1)}, u32[]{:S(2)}, u32[]{:S(2)}) collective-permute-start(bf16[128,128]{1,0:T(8,128)(2,1)S(1)} %collective-permute-done.7), channel_id=1, source_target_pairs={{0,15},{1,0},{2,1},{3,2},{4,3},{5,4},{6,5},{7,6},{8,7},{9,8},{10,9... | collective-permute-start | bytes 98312 | tf_op jit(solution)/shard_map/ppermute | solution.py:20
  50.2 6.7 %collective-permute-start.11 = (bf16[128,128]{1,0:T(8,128)(2,1)S(1)}, bf16[128,128]{1,0:T(8,128)(2,1)S(1)}, u32[]{:S(2)}, u32[]{:S(2)}) collective-permute-start(bf16[128,128]{1,0:T(8,128)(2,1)S(1)} %collective-permute-done.9), channel_id=1, source_target_pairs={{0,15},{1,0},{2,1},{3,2},{4,3},{5,4},{6,5},{7,6},{8,7},{9,8},{10,9... | collective-permute-start | bytes 98312 | tf_op jit(solution)/shard_map/ppermute | solution.py:20
  58.9 6.7 %collective-permute-start.13 = (bf16[128,128]{1,0:T(8,128)(2,1)S(1)}, bf16[128,128]{1,0:T(8,128)(2,1)S(1)}, u32[]{:S(2)}, u32[]{:S(2)}) collective-permute-start(bf16[128,128]{1,0:T(8,128)(2,1)S(1)} %collective-permute-done.11), channel_id=1, source_target_pairs={{0,15},{1,0},{2,1},{3,2},{4,3},{5,4},{6,5},{7,6},{8,7},{9,8},{10,9... | collective-permute-start | bytes 98312 | tf_op jit(solution)/shard_map/ppermute | solution.py:20
  67.6 6.0 %collective-permute-done.14 = bf16[128,128]{1,0:T(8,128)(2,1)S(1)} collective-permute-done((bf16[128,128]{1,0:T(8,128)(2,1)S(1)}, bf16[128,128]{1,0:T(8,128)(2,1)S(1)}, u32[]{:S(2)}, u32[]{:S(2)}) %collective-permute-start.14) | collective-permute-done | bytes 32800 | tf_op jit(solution)/shard_map/ppermute | solution.py:17
  80.2 20.8 %all-to-all-start = ((f32[32,56,128]{2,1,0:T(8,128)}), f32[32,56,128]{2,1,0:T(8,128)S(1)}, u32[]{:S(2)}, u32[]{:S(2)}) async-start(f32[32,56,128]{2,1,0:T(8,128)} %bitcast.7), calls=%async_computation | async-start | bytes 1835008 | tf_op jit(solution)/shard_map/all_to_all | solution.py:30
  101.1 50.2 %all-to-all-done = f32[32,56,128]{2,1,0:T(8,128)S(1)} async-done(((f32[32,56,128]{2,1,0:T(8,128)}), f32[32,56,128]{2,1,0:T(8,128)S(1)}, u32[]{:S(2)}, u32[]{:S(2)}) %all-to-all-start) | async-done | bytes 917536 | tf_op jit(solution)/shard_map/all_to_all | solution.py:30
  151.3 29.7 %all_gather.9 = f32[1792,128]{1,0:T(8,128)S(1)} all-gather(f32[56,128]{1,0:T(8,128)S(1)} %reduce_sum.137), channel_id=1, replica_groups=mesh['comp'=32,'feat'=16] {'comp'}, dimensions={0}, use_global_device_ids=true | all-gather | bytes 946176 | tf_op jit(solution)/shard_map/all_gather | solution.py:95
  188.1 3.8 all-to-all-start.1
  191.9 17.4 %all-to-all-done.1 = f32[16,128,128]{2,1,0:T(8,128)S(1)} async-done(((f32[16,128,128]{2,1,0:T(8,128)}), f32[16,128,128]{2,1,0:T(8,128)S(1)}, u32[]{:S(2)}, u32[]{:S(2)}) %all-to-all-start.1) | async-done | bytes 1048608 | tf_op jit(solution)/shard_map/all_to_all | solution.py:30
  209.4 9.5 %all_to_all.45 = f32[16,2,128]{2,1,0:T(2,128)S(1)} all-to-all(f32[16,2,128]{2,1,0:T(2,128)S(1)} %broadcast_in_dim.30), channel_id=1, replica_groups=mesh['comp'=32,'feat'=16] {'feat'}, dimensions={0} | all-to-all | bytes 32768 | tf_op jit(solution)/shard_map/all_to_all | solution.py:35
  219.0 19.3 %all_to_all.46 = f32[32,2,128]{2,1,0:T(2,128)S(1)} all-to-all(f32[32,2,128]{2,1,0:T(2,128)S(1)} %broadcast_in_dim.31), channel_id=1, replica_groups=mesh['comp'=32,'feat'=16] {'comp'}, dimensions={0} | all-to-all | bytes 65536 | tf_op jit(solution)/shard_map/all_to_all | solution.py:37
  240.7 6.4 %collective-permute-start.16 = (bf16[128,128]{1,0:T(8,128)(2,1)S(1)}, bf16[128,128]{1,0:T(8,128)(2,1)S(1)}, u32[]{:S(2)}, u32[]{:S(2)}) collective-permute-start(bf16[128,128]{1,0:T(8,128)(2,1)S(1)} %get-tuple-element.9), channel_id=1, source_target_pairs={{0,15},{1,0},{2,1},{3,2},{4,3},{5,4},{6,5},{7,6},{8,7},{9,8},{10,9... | collective-permute-start | bytes 98312 | tf_op jit(solution)/shard_map/ppermute | solution.py:20
  249.1 6.7 %collective-permute-start.18 = (bf16[128,128]{1,0:T(8,128)(2,1)S(1)}, bf16[128,128]{1,0:T(8,128)(2,1)S(1)}, u32[]{:S(2)}, u32[]{:S(2)}) collective-permute-start(bf16[128,128]{1,0:T(8,128)(2,1)S(1)} %collective-permute-done.16), channel_id=1, source_target_pairs={{0,15},{1,0},{2,1},{3,2},{4,3},{5,4},{6,5},{7,6},{8,7},{9,8},{10,9... | collective-permute-start | bytes 98312 | tf_op jit(solution)/shard_map/ppermute | solution.py:20
  257.8 6.7 %collective-permute-start.20 = (bf16[128,128]{1,0:T(8,128)(2,1)S(1)}, bf16[128,128]{1,0:T(8,128)(2,1)S(1)}, u32[]{:S(2)}, u32[]{:S(2)}) collective-permute-start(bf16[128,128]{1,0:T(8,128)(2,1)S(1)} %collective-permute-done.18), channel_id=1, source_target_pairs={{0,15},{1,0},{2,1},{3,2},{4,3},{5,4},{6,5},{7,6},{8,7},{9,8},{10,9... | collective-permute-start | bytes 98312 | tf_op jit(solution)/shard_map/ppermute | solution.py:20
  266.5 6.7 %collective-permute-start.22 = (bf16[128,128]{1,0:T(8,128)(2,1)S(1)}, bf16[128,128]{1,0:T(8,128)(2,1)S(1)}, u32[]{:S(2)}, u32[]{:S(2)}) collective-permute-start(bf16[128,128]{1,0:T(8,128)(2,1)S(1)} %collective-permute-done.20), channel_id=1, source_target_pairs={{0,15},{1,0},{2,1},{3,2},{4,3},{5,4},{6,5},{7,6},{8,7},{9,8},{10,9... | collective-permute-start | bytes 98312 | tf_op jit(solution)/shard_map/ppermute | solution.py:20
  275.1 6.7 %collective-permute-start.24 = (bf16[128,128]{1,0:T(8,128)(2,1)S(1)}, bf16[128,128]{1,0:T(8,128)(2,1)S(1)}, u32[]{:S(2)}, u32[]{:S(2)}) collective-permute-start(bf16[128,128]{1,0:T(8,128)(2,1)S(1)} %collective-permute-done.22), channel_id=1, source_target_pairs={{0,15},{1,0},{2,1},{3,2},{4,3},{5,4},{6,5},{7,6},{8,7},{9,8},{10,9... | collective-permute-start | bytes 98312 | tf_op jit(solution)/shard_map/ppermute | solution.py:20
  283.8 6.7 %collective-permute-start.26 = (bf16[128,128]{1,0:T(8,128)(2,1)S(1)}, bf16[128,128]{1,0:T(8,128)(2,1)S(1)}, u32[]{:S(2)}, u32[]{:S(2)}) collective-permute-start(bf16[128,128]{1,0:T(8,128)(2,1)S(1)} %collective-permute-done.24), channel_id=1, source_target_pairs={{0,15},{1,0},{2,1},{3,2},{4,3},{5,4},{6,5},{7,6},{8,7},{9,8},{10,9... | collective-permute-start | bytes 98312 | tf_op jit(solution)/shard_map/ppermute | solution.py:20
  292.5 6.7 %collective-permute-start.28 = (bf16[128,128]{1,0:T(8,128)(2,1)S(1)}, bf16[128,128]{1,0:T(8,128)(2,1)S(1)}, u32[]{:S(2)}, u32[]{:S(2)}) collective-permute-start(bf16[128,128]{1,0:T(8,128)(2,1)S(1)} %collective-permute-done.26), channel_id=1, source_target_pairs={{0,15},{1,0},{2,1},{3,2},{4,3},{5,4},{6,5},{7,6},{8,7},{9,8},{10,9... | collective-permute-start | bytes 98312 | tf_op jit(solution)/shard_map/ppermute | solution.py:20
  301.4 5.8 %collective-permute-done.29 = bf16[128,128]{1,0:T(8,128)(2,1)S(1)} collective-permute-done((bf16[128,128]{1,0:T(8,128)(2,1)S(1)}, bf16[128,128]{1,0:T(8,128)(2,1)S(1)}, u32[]{:S(2)}, u32[]{:S(2)}) %collective-permute-start.29) | collective-permute-done | bytes 32800 | tf_op jit(solution)/shard_map/ppermute | solution.py:17
  313.8 9.8 %all-to-all-start.4 = ((f32[32,56,128]{2,1,0:T(8,128)}), f32[32,56,128]{2,1,0:T(8,128)S(1)}, u32[]{:S(2)}, u32[]{:S(2)}) async-start(f32[32,56,128]{2,1,0:T(8,128)} %bitcast.17), calls=%async_computation.4 | async-start | bytes 1835008 | tf_op jit(solution)/shard_map/all_to_all | solution.py:30
  324.5 49.3 %all-to-all-done.4 = f32[32,56,128]{2,1,0:T(8,128)S(1)} async-done(((f32[32,56,128]{2,1,0:T(8,128)}), f32[32,56,128]{2,1,0:T(8,128)S(1)}, u32[]{:S(2)}, u32[]{:S(2)}) %all-to-all-start.4) | async-done | bytes 917536 | tf_op jit(solution)/shard_map/all_to_all | solution.py:30
  374.7 30.6 %all-gather.1 = f32[32,57,128]{2,1,0:T(8,128)S(1)} all-gather(f32[1,57,128]{2,1,0:T(8,128)S(1)} %maximum_bitcast_fusion), channel_id=2, replica_groups=mesh['comp'=32,'feat'=16] {'comp'}, dimensions={0}, use_global_device_ids=true | all-gather | bytes 963072 | tf_op jit(solution)/shard_map/all_gather | solution.py:105
  410.4 5.3 %all-to-all-done.5 = f32[16,1,128]{2,1,0:T(1,128)S(1)} async-done(((f32[16,1,128]{2,1,0:T(1,128)}), f32[16,1,128]{2,1,0:T(1,128)S(1)}, u32[]{:S(2)}, u32[]{:S(2)}) %all-to-all-start.5) | async-done | bytes 8224 | tf_op jit(solution)/shard_map/all_to_all | solution.py:114
  424.9 3.7 all-to-all-start.6
  429.3 14.5 %all-to-all-done.6 = f32[16,128,128]{2,1,0:T(8,128)S(1)} async-done(((f32[16,128,128]{2,1,0:T(8,128)}), f32[16,128,128]{2,1,0:T(8,128)S(1)}, u32[]{:S(2)}, u32[]{:S(2)}) %all-to-all-start.6) | async-done | bytes 1048608 | tf_op jit(solution)/shard_map/all_to_all | solution.py:30
  443.9 10.1 %all_to_all.47 = f32[16,2,128]{2,1,0:T(2,128)S(1)} all-to-all(f32[16,2,128]{2,1,0:T(2,128)S(1)} %broadcast_in_dim.34), channel_id=1, replica_groups=mesh['comp'=32,'feat'=16] {'feat'}, dimensions={0} | all-to-all | bytes 32768 | tf_op jit(solution)/shard_map/all_to_all | solution.py:35
  454.1 19.7 %all_to_all.48 = f32[32,2,128]{2,1,0:T(2,128)S(1)} all-to-all(f32[32,2,128]{2,1,0:T(2,128)S(1)} %broadcast_in_dim.35), channel_id=1, replica_groups=mesh['comp'=32,'feat'=16] {'comp'}, dimensions={0} | all-to-all | bytes 65536 | tf_op jit(solution)/shard_map/all_to_all | solution.py:37
  (146 shorter events, 72.7 us)
Async XLA Ops:
  1.6 11.9 %collective-permute-start = (bf16[128,128]{1,0:T(8,128)(2,1)S(1)}, bf16[128,128]{1,0:T(8,128)(2,1)S(1)}, u32[]{:S(2)}, u32[]{:S(2)}) collective-permute-start(bf16[128,128]{1,0:T(8,128)(2,1)S(1)} %get-tuple-element.11), channel_id=1, source_target_pairs={{0,1},{1,2},{2,3},{3,4},{4,5},{5,6},{6,7},{7,8},{8,9},{9,10},{10,1... | collective-permute-start | bytes 98312 | tf_op jit(solution)/shard_map/ppermute | solution.py:17
  5.7 9.8 %collective-permute-start.1 = (bf16[128,128]{1,0:T(8,128)(2,1)S(1)}, bf16[128,128]{1,0:T(8,128)(2,1)S(1)}, u32[]{:S(2)}, u32[]{:S(2)}) collective-permute-start(bf16[128,128]{1,0:T(8,128)(2,1)S(1)} %get-tuple-element.11), channel_id=1, source_target_pairs={{0,15},{1,0},{2,1},{3,2},{4,3},{5,4},{6,5},{7,6},{8,7},{9,8},{10,9... | collective-permute-start | bytes 98312 | tf_op jit(solution)/shard_map/ppermute | solution.py:20
  13.5 8.7 %collective-permute-start.2 = (bf16[128,128]{1,0:T(8,128)(2,1)S(1)}, bf16[128,128]{1,0:T(8,128)(2,1)S(1)}, u32[]{:S(2)}, u32[]{:S(2)}) collective-permute-start(bf16[128,128]{1,0:T(8,128)(2,1)S(1)} %collective-permute-done), channel_id=1, source_target_pairs={{0,1},{1,2},{2,3},{3,4},{4,5},{5,6},{6,7},{7,8},{8,9},{9,10},{10,1... | collective-permute-start | bytes 98312 | tf_op jit(solution)/shard_map/ppermute | solution.py:17
  15.5 8.7 %collective-permute-start.3 = (bf16[128,128]{1,0:T(8,128)(2,1)S(1)}, bf16[128,128]{1,0:T(8,128)(2,1)S(1)}, u32[]{:S(2)}, u32[]{:S(2)}) collective-permute-start(bf16[128,128]{1,0:T(8,128)(2,1)S(1)} %collective-permute-done.1), channel_id=1, source_target_pairs={{0,15},{1,0},{2,1},{3,2},{4,3},{5,4},{6,5},{7,6},{8,7},{9,8},{10,9... | collective-permute-start | bytes 98312 | tf_op jit(solution)/shard_map/ppermute | solution.py:20
  22.2 8.7 %collective-permute-start.4 = (bf16[128,128]{1,0:T(8,128)(2,1)S(1)}, bf16[128,128]{1,0:T(8,128)(2,1)S(1)}, u32[]{:S(2)}, u32[]{:S(2)}) collective-permute-start(bf16[128,128]{1,0:T(8,128)(2,1)S(1)} %collective-permute-done.2), channel_id=1, source_target_pairs={{0,1},{1,2},{2,3},{3,4},{4,5},{5,6},{6,7},{7,8},{8,9},{9,10},{10,1... | collective-permute-start | bytes 98312 | tf_op jit(solution)/shard_map/ppermute | solution.py:17
  24.2 8.7 %collective-permute-start.5 = (bf16[128,128]{1,0:T(8,128)(2,1)S(1)}, bf16[128,128]{1,0:T(8,128)(2,1)S(1)}, u32[]{:S(2)}, u32[]{:S(2)}) collective-permute-start(bf16[128,128]{1,0:T(8,128)(2,1)S(1)} %collective-permute-done.3), channel_id=1, source_target_pairs={{0,15},{1,0},{2,1},{3,2},{4,3},{5,4},{6,5},{7,6},{8,7},{9,8},{10,9... | collective-permute-start | bytes 98312 | tf_op jit(solution)/shard_map/ppermute | solution.py:20
  30.9 8.7 %collective-permute-start.6 = (bf16[128,128]{1,0:T(8,128)(2,1)S(1)}, bf16[128,128]{1,0:T(8,128)(2,1)S(1)}, u32[]{:S(2)}, u32[]{:S(2)}) collective-permute-start(bf16[128,128]{1,0:T(8,128)(2,1)S(1)} %collective-permute-done.4), channel_id=1, source_target_pairs={{0,1},{1,2},{2,3},{3,4},{4,5},{5,6},{6,7},{7,8},{8,9},{9,10},{10,1... | collective-permute-start | bytes 98312 | tf_op jit(solution)/shard_map/ppermute | solution.py:17
  32.8 8.7 %collective-permute-start.7 = (bf16[128,128]{1,0:T(8,128)(2,1)S(1)}, bf16[128,128]{1,0:T(8,128)(2,1)S(1)}, u32[]{:S(2)}, u32[]{:S(2)}) collective-permute-start(bf16[128,128]{1,0:T(8,128)(2,1)S(1)} %collective-permute-done.5), channel_id=1, source_target_pairs={{0,15},{1,0},{2,1},{3,2},{4,3},{5,4},{6,5},{7,6},{8,7},{9,8},{10,9... | collective-permute-start | bytes 98312 | tf_op jit(solution)/shard_map/ppermute | solution.py:20
  39.6 8.7 %collective-permute-start.8 = (bf16[128,128]{1,0:T(8,128)(2,1)S(1)}, bf16[128,128]{1,0:T(8,128)(2,1)S(1)}, u32[]{:S(2)}, u32[]{:S(2)}) collective-permute-start(bf16[128,128]{1,0:T(8,128)(2,1)S(1)} %collective-permute-done.6), channel_id=1, source_target_pairs={{0,1},{1,2},{2,3},{3,4},{4,5},{5,6},{6,7},{7,8},{8,9},{9,10},{10,1... | collective-permute-start | bytes 98312 | tf_op jit(solution)/shard_map/ppermute | solution.py:17
  41.5 8.7 %collective-permute-start.9 = (bf16[128,128]{1,0:T(8,128)(2,1)S(1)}, bf16[128,128]{1,0:T(8,128)(2,1)S(1)}, u32[]{:S(2)}, u32[]{:S(2)}) collective-permute-start(bf16[128,128]{1,0:T(8,128)(2,1)S(1)} %collective-permute-done.7), channel_id=1, source_target_pairs={{0,15},{1,0},{2,1},{3,2},{4,3},{5,4},{6,5},{7,6},{8,7},{9,8},{10,9... | collective-permute-start | bytes 98312 | tf_op jit(solution)/shard_map/ppermute | solution.py:20
  48.3 8.7 %collective-permute-start.10 = (bf16[128,128]{1,0:T(8,128)(2,1)S(1)}, bf16[128,128]{1,0:T(8,128)(2,1)S(1)}, u32[]{:S(2)}, u32[]{:S(2)}) collective-permute-start(bf16[128,128]{1,0:T(8,128)(2,1)S(1)} %collective-permute-done.8), channel_id=1, source_target_pairs={{0,1},{1,2},{2,3},{3,4},{4,5},{5,6},{6,7},{7,8},{8,9},{9,10},{10,1... | collective-permute-start | bytes 98312 | tf_op jit(solution)/shard_map/ppermute | solution.py:17
  50.2 8.7 %collective-permute-start.11 = (bf16[128,128]{1,0:T(8,128)(2,1)S(1)}, bf16[128,128]{1,0:T(8,128)(2,1)S(1)}, u32[]{:S(2)}, u32[]{:S(2)}) collective-permute-start(bf16[128,128]{1,0:T(8,128)(2,1)S(1)} %collective-permute-done.9), channel_id=1, source_target_pairs={{0,15},{1,0},{2,1},{3,2},{4,3},{5,4},{6,5},{7,6},{8,7},{9,8},{10,9... | collective-permute-start | bytes 98312 | tf_op jit(solution)/shard_map/ppermute | solution.py:20
  56.9 8.7 %collective-permute-start.12 = (bf16[128,128]{1,0:T(8,128)(2,1)S(1)}, bf16[128,128]{1,0:T(8,128)(2,1)S(1)}, u32[]{:S(2)}, u32[]{:S(2)}) collective-permute-start(bf16[128,128]{1,0:T(8,128)(2,1)S(1)} %collective-permute-done.10), channel_id=1, source_target_pairs={{0,1},{1,2},{2,3},{3,4},{4,5},{5,6},{6,7},{7,8},{8,9},{9,10},{10,1... | collective-permute-start | bytes 98312 | tf_op jit(solution)/shard_map/ppermute | solution.py:17
  58.9 8.7 %collective-permute-start.13 = (bf16[128,128]{1,0:T(8,128)(2,1)S(1)}, bf16[128,128]{1,0:T(8,128)(2,1)S(1)}, u32[]{:S(2)}, u32[]{:S(2)}) collective-permute-start(bf16[128,128]{1,0:T(8,128)(2,1)S(1)} %collective-permute-done.11), channel_id=1, source_target_pairs={{0,15},{1,0},{2,1},{3,2},{4,3},{5,4},{6,5},{7,6},{8,7},{9,8},{10,9... | collective-permute-start | bytes 98312 | tf_op jit(solution)/shard_map/ppermute | solution.py:20
  80.2 71.0 %all-to-all-start = ((f32[32,56,128]{2,1,0:T(8,128)}), f32[32,56,128]{2,1,0:T(8,128)S(1)}, u32[]{:S(2)}, u32[]{:S(2)}) async-start(f32[32,56,128]{2,1,0:T(8,128)} %bitcast.7), calls=%async_computation | async-start | bytes 1835008 | tf_op jit(solution)/shard_map/all_to_all | solution.py:30
  188.1 21.2 %all-to-all-start.1 = ((f32[16,128,128]{2,1,0:T(8,128)}), f32[16,128,128]{2,1,0:T(8,128)S(1)}, u32[]{:S(2)}, u32[]{:S(2)}) async-start(f32[16,128,128]{2,1,0:T(8,128)} %copy.47), calls=%async_computation.1 | async-start | bytes 2097152 | tf_op jit(solution)/shard_map/all_to_all | solution.py:30
  238.5 8.6 %collective-permute-start.15 = (bf16[128,128]{1,0:T(8,128)(2,1)S(1)}, bf16[128,128]{1,0:T(8,128)(2,1)S(1)}, u32[]{:S(2)}, u32[]{:S(2)}) collective-permute-start(bf16[128,128]{1,0:T(8,128)(2,1)S(1)} %get-tuple-element.9), channel_id=1, source_target_pairs={{0,1},{1,2},{2,3},{3,4},{4,5},{5,6},{6,7},{7,8},{8,9},{9,10},{10,1... | collective-permute-start | bytes 98312 | tf_op jit(solution)/shard_map/ppermute | solution.py:17
  247.1 8.7 %collective-permute-start.17 = (bf16[128,128]{1,0:T(8,128)(2,1)S(1)}, bf16[128,128]{1,0:T(8,128)(2,1)S(1)}, u32[]{:S(2)}, u32[]{:S(2)}) collective-permute-start(bf16[128,128]{1,0:T(8,128)(2,1)S(1)} %collective-permute-done.15), channel_id=1, source_target_pairs={{0,1},{1,2},{2,3},{3,4},{4,5},{5,6},{6,7},{7,8},{8,9},{9,10},{10,1... | collective-permute-start | bytes 98312 | tf_op jit(solution)/shard_map/ppermute | solution.py:17
  249.1 8.7 %collective-permute-start.18 = (bf16[128,128]{1,0:T(8,128)(2,1)S(1)}, bf16[128,128]{1,0:T(8,128)(2,1)S(1)}, u32[]{:S(2)}, u32[]{:S(2)}) collective-permute-start(bf16[128,128]{1,0:T(8,128)(2,1)S(1)} %collective-permute-done.16), channel_id=1, source_target_pairs={{0,15},{1,0},{2,1},{3,2},{4,3},{5,4},{6,5},{7,6},{8,7},{9,8},{10,9... | collective-permute-start | bytes 98312 | tf_op jit(solution)/shard_map/ppermute | solution.py:20
  255.8 8.7 %collective-permute-start.19 = (bf16[128,128]{1,0:T(8,128)(2,1)S(1)}, bf16[128,128]{1,0:T(8,128)(2,1)S(1)}, u32[]{:S(2)}, u32[]{:S(2)}) collective-permute-start(bf16[128,128]{1,0:T(8,128)(2,1)S(1)} %collective-permute-done.17), channel_id=1, source_target_pairs={{0,1},{1,2},{2,3},{3,4},{4,5},{5,6},{6,7},{7,8},{8,9},{9,10},{10,1... | collective-permute-start | bytes 98312 | tf_op jit(solution)/shard_map/ppermute | solution.py:17
  257.8 8.7 %collective-permute-start.20 = (bf16[128,128]{1,0:T(8,128)(2,1)S(1)}, bf16[128,128]{1,0:T(8,128)(2,1)S(1)}, u32[]{:S(2)}, u32[]{:S(2)}) collective-permute-start(bf16[128,128]{1,0:T(8,128)(2,1)S(1)} %collective-permute-done.18), channel_id=1, source_target_pairs={{0,15},{1,0},{2,1},{3,2},{4,3},{5,4},{6,5},{7,6},{8,7},{9,8},{10,9... | collective-permute-start | bytes 98312 | tf_op jit(solution)/shard_map/ppermute | solution.py:20
  264.5 8.7 %collective-permute-start.21 = (bf16[128,128]{1,0:T(8,128)(2,1)S(1)}, bf16[128,128]{1,0:T(8,128)(2,1)S(1)}, u32[]{:S(2)}, u32[]{:S(2)}) collective-permute-start(bf16[128,128]{1,0:T(8,128)(2,1)S(1)} %collective-permute-done.19), channel_id=1, source_target_pairs={{0,1},{1,2},{2,3},{3,4},{4,5},{5,6},{6,7},{7,8},{8,9},{9,10},{10,1... | collective-permute-start | bytes 98312 | tf_op jit(solution)/shard_map/ppermute | solution.py:17
  266.5 8.7 %collective-permute-start.22 = (bf16[128,128]{1,0:T(8,128)(2,1)S(1)}, bf16[128,128]{1,0:T(8,128)(2,1)S(1)}, u32[]{:S(2)}, u32[]{:S(2)}) collective-permute-start(bf16[128,128]{1,0:T(8,128)(2,1)S(1)} %collective-permute-done.20), channel_id=1, source_target_pairs={{0,15},{1,0},{2,1},{3,2},{4,3},{5,4},{6,5},{7,6},{8,7},{9,8},{10,9... | collective-permute-start | bytes 98312 | tf_op jit(solution)/shard_map/ppermute | solution.py:20
  273.2 8.7 %collective-permute-start.23 = (bf16[128,128]{1,0:T(8,128)(2,1)S(1)}, bf16[128,128]{1,0:T(8,128)(2,1)S(1)}, u32[]{:S(2)}, u32[]{:S(2)}) collective-permute-start(bf16[128,128]{1,0:T(8,128)(2,1)S(1)} %collective-permute-done.21), channel_id=1, source_target_pairs={{0,1},{1,2},{2,3},{3,4},{4,5},{5,6},{6,7},{7,8},{8,9},{9,10},{10,1... | collective-permute-start | bytes 98312 | tf_op jit(solution)/shard_map/ppermute | solution.py:17
  275.1 8.7 %collective-permute-start.24 = (bf16[128,128]{1,0:T(8,128)(2,1)S(1)}, bf16[128,128]{1,0:T(8,128)(2,1)S(1)}, u32[]{:S(2)}, u32[]{:S(2)}) collective-permute-start(bf16[128,128]{1,0:T(8,128)(2,1)S(1)} %collective-permute-done.22), channel_id=1, source_target_pairs={{0,15},{1,0},{2,1},{3,2},{4,3},{5,4},{6,5},{7,6},{8,7},{9,8},{10,9... | collective-permute-start | bytes 98312 | tf_op jit(solution)/shard_map/ppermute | solution.py:20
  281.9 8.7 %collective-permute-start.25 = (bf16[128,128]{1,0:T(8,128)(2,1)S(1)}, bf16[128,128]{1,0:T(8,128)(2,1)S(1)}, u32[]{:S(2)}, u32[]{:S(2)}) collective-permute-start(bf16[128,128]{1,0:T(8,128)(2,1)S(1)} %collective-permute-done.23), channel_id=1, source_target_pairs={{0,1},{1,2},{2,3},{3,4},{4,5},{5,6},{6,7},{7,8},{8,9},{9,10},{10,1... | collective-permute-start | bytes 98312 | tf_op jit(solution)/shard_map/ppermute | solution.py:17
  283.8 8.7 %collective-permute-start.26 = (bf16[128,128]{1,0:T(8,128)(2,1)S(1)}, bf16[128,128]{1,0:T(8,128)(2,1)S(1)}, u32[]{:S(2)}, u32[]{:S(2)}) collective-permute-start(bf16[128,128]{1,0:T(8,128)(2,1)S(1)} %collective-permute-done.24), channel_id=1, source_target_pairs={{0,15},{1,0},{2,1},{3,2},{4,3},{5,4},{6,5},{7,6},{8,7},{9,8},{10,9... | collective-permute-start | bytes 98312 | tf_op jit(solution)/shard_map/ppermute | solution.py:20
  290.5 8.7 %collective-permute-start.27 = (bf16[128,128]{1,0:T(8,128)(2,1)S(1)}, bf16[128,128]{1,0:T(8,128)(2,1)S(1)}, u32[]{:S(2)}, u32[]{:S(2)}) collective-permute-start(bf16[128,128]{1,0:T(8,128)(2,1)S(1)} %collective-permute-done.25), channel_id=1, source_target_pairs={{0,1},{1,2},{2,3},{3,4},{4,5},{5,6},{6,7},{7,8},{8,9},{9,10},{10,1... | collective-permute-start | bytes 98312 | tf_op jit(solution)/shard_map/ppermute | solution.py:17
  292.5 8.9 %collective-permute-start.28 = (bf16[128,128]{1,0:T(8,128)(2,1)S(1)}, bf16[128,128]{1,0:T(8,128)(2,1)S(1)}, u32[]{:S(2)}, u32[]{:S(2)}) collective-permute-start(bf16[128,128]{1,0:T(8,128)(2,1)S(1)} %collective-permute-done.26), channel_id=1, source_target_pairs={{0,15},{1,0},{2,1},{3,2},{4,3},{5,4},{6,5},{7,6},{8,7},{9,8},{10,9... | collective-permute-start | bytes 98312 | tf_op jit(solution)/shard_map/ppermute | solution.py:20
  313.8 60.0 %all-to-all-start.4 = ((f32[32,56,128]{2,1,0:T(8,128)}), f32[32,56,128]{2,1,0:T(8,128)S(1)}, u32[]{:S(2)}, u32[]{:S(2)}) async-start(f32[32,56,128]{2,1,0:T(8,128)} %bitcast.17), calls=%async_computation.4 | async-start | bytes 1835008 | tf_op jit(solution)/shard_map/all_to_all | solution.py:30
  405.9 9.8 %all-to-all-start.5 = ((f32[16,1,128]{2,1,0:T(1,128)}), f32[16,1,128]{2,1,0:T(1,128)S(1)}, u32[]{:S(2)}, u32[]{:S(2)}) async-start(f32[16,1,128]{2,1,0:T(1,128)} %broadcast_in_dim.33), calls=%async_computation.5 | async-start | bytes 16384 | tf_op jit(solution)/shard_map/all_to_all | solution.py:114
  424.9 18.9 %all-to-all-start.6 = ((f32[16,128,128]{2,1,0:T(8,128)}), f32[16,128,128]{2,1,0:T(8,128)S(1)}, u32[]{:S(2)}, u32[]{:S(2)}) async-start(f32[16,128,128]{2,1,0:T(8,128)} %copy.56), calls=%async_computation.6 | async-start | bytes 2097152 | tf_op jit(solution)/shard_map/all_to_all | solution.py:30
  (8 other events, 202.6 us)
